TPU v7x, 256 devices: a whole 4x4x8 slice. The times are simulated.
256 devices in a mesh: seq: 16 (over y, z_hi, core), head: 16 (over x, z_lo).
Axes of the slice: x: 4, y: 4, z: 8 (z_hi: 2, z_lo: 4; z = z_hi * 4 + z_lo), core: 2. Of those that a mesh axis runs over, the one named last changes fastest.
Arguments:
- x_in: bfloat16 [8192, 8192], P('seq', 'head'), may hold values from -6 to 6
- z_in: bfloat16 [8192, 8192], P('seq', 'head'), may hold values from -12 to 12
- bc: bfloat16 [2, 8192, 128], P(None, 'seq'), may hold values from -1.796875 to 1.796875
- dt_raw: float32 [128, 8192], P('head', 'seq'), may hold values from -3 to 3
- dt_bias: float32 [128], P('head'), may hold values from -8 to 0
- decay_rate: float32 [128], P('head'), may hold values from 0.001 to 0.4
- d_skip: float32 [128], P('head'), may hold values from 0.5 to 1.5
- norm_gain: float32 [8192], P('head'), may hold values from 0.1 to 1.9
- out_weight: bfloat16 [8192, 4096], P('head', 'seq'), may hold values from -0.0625 to 0.0625
- resid: bfloat16 [8192, 4096], P(('seq', 'head')), may hold values from -6 to 6
- mlp_gain: float32 [4096], replicated, may hold values from 0.1 to 1.9
- gate_weight: bfloat16 [4096, 8192], P(None, 'head'), may hold values from -0.09375 to 0.09375
- up_weight: bfloat16 [4096, 8192], P(None, 'head'), may hold values from -0.09375 to 0.09375
- down_weight: bfloat16 [8192, 4096], P('head', 'seq'), may hold values from -0.0625 to 0.0625
Outputs:
- layer_out: bfloat16 [8192, 4096], P(('seq', 'head'))
All inputs are finite; a program needn't handle non-finite values.
Results may differ from a plain program's by a relative error of at most 0.0075.
Values may be sent and summed in bfloat16 or wider, within the bound.
No kernel may reach another device: no remote copies, remote signals or barrier semaphores. Data moves between devices by JAX's collectives and lax.ppermute only.
A program may use at most 128 MiB of HBM per device.

v0:
```python
import jax
import jax.numpy as jnp
from jax import lax
from jax.sharding import PartitionSpec as P

BLOCK = 256
INNER = 8192
epsilon = 1e-05


def passed_along(value, axis, steps):
    count = lax.axis_size(axis)
    initial, last = (max(0, -steps), min(count, count - steps))
    return lax.ppermute(value, axis, [(source, source + steps) for source in range(initial, last)])


def block_scan(x_heads, b_rows, c_rows, step_size, log_decay, block_len, start_state):
    length, head_count, head_width = x_heads.shape
    state_size = b_rows.shape[1]
    block_count = length // block_len
    x_blocks = x_heads.reshape(block_count, block_len, head_count, head_width)
    b_blocks = b_rows.reshape(block_count, block_len, state_size)
    c_blocks = c_rows.reshape(block_count, block_len, state_size)
    d_blocks = step_size.reshape(head_count, block_count, block_len).transpose(1, 0, 2)
    a_blocks = log_decay.reshape(head_count, block_count, block_len).transpose(1, 0, 2)
    lower_mask = jnp.tril(jnp.ones((block_len, block_len), dtype=bool))

    def advance(carry_state, inputs):
        x_block, b_block, c_block, d_block, a_block = inputs
        cumulative = jnp.cumsum(a_block, axis=1)
        gap_values = jnp.where(
            lower_mask[None], cumulative[:, :, None] - cumulative[:, None, :], -jnp.inf
        )
        scores = jnp.dot(c_block, b_block.T, preferred_element_type=jnp.float32)
        mixing = (jnp.exp(gap_values) * scores[None] * d_block[:, None, :]).astype(jnp.bfloat16)
        within = jnp.einsum("hij,jhp->ihp", mixing, x_block, preferred_element_type=jnp.float32)
        carried = jnp.einsum(
            "in,hpn->ihp", c_block.astype(jnp.float32), carry_state, precision=lax.Precision.HIGHEST
        )
        carried = carried * jnp.exp(cumulative).T[:, :, None]
        last_cum = cumulative[:, -1:]
        inject = (
            (jnp.exp(last_cum - cumulative) * d_block)[:, :, None]
            * b_block.astype(jnp.float32)[None]
        ).astype(jnp.bfloat16)
        added = jnp.einsum("jhp,hjn->hpn", x_block, inject, preferred_element_type=jnp.float32)
        new_state = jnp.exp(last_cum)[:, :, None] * carry_state + added
        return (new_state, within + carried)

    final_state, block_outs = lax.scan(
        advance, start_state, (x_blocks, b_blocks, c_blocks, d_blocks, a_blocks)
    )
    return (block_outs.reshape(length, head_count, head_width), final_state)


def normalize_rows(layer_sum, mlp_gain):
    mean_square = jnp.mean(layer_sum * layer_sum, axis=1, keepdims=True)
    return (layer_sum * lax.rsqrt(mean_square + epsilon) * mlp_gain).astype(jnp.bfloat16)


def shards(
    x_in,
    z_in,
    bc,
    dt_raw,
    dt_bias,
    decay_rate,
    d_skip,
    norm_gain,
    out_weight,
    resid,
    mlp_gain,
    gate_weight,
    up_weight,
    down_weight,
):
    out_full, down_full = (
        lax.all_gather(out_weight, "seq", axis=1, tiled=True),
        lax.all_gather(down_weight, "seq", axis=1, tiled=True),
    )
    head_count = dt_raw.shape[0]
    length = dt_raw.shape[1]
    head_width = x_in.shape[1] // head_count
    state_size = bc.shape[2]
    step_size = jax.nn.softplus(dt_raw + dt_bias[:, None])
    log_decay = -decay_rate[:, None] * step_size
    x_heads = x_in.reshape(length, head_count, head_width)
    zero_state = jnp.zeros((head_count, head_width, state_size), jnp.float32)
    local_out, local_state = block_scan(
        x_heads, bc[0], bc[1], step_size, log_decay, BLOCK, zero_state
    )
    running = jnp.cumsum(log_decay, axis=1)
    group_decay = jnp.exp(running[:, -1])

    def relay_step(relay_turn, incoming):
        outgoing = group_decay[:, None, None] * incoming + local_state
        return passed_along(outgoing, "seq", 1)

    entering = lax.fori_loop(0, lax.axis_size("seq") - 1, relay_step, zero_state)
    carried = jnp.einsum(
        "tn,hpn->thp", bc[1].astype(jnp.float32), entering, precision=lax.Precision.HIGHEST
    )
    carried = carried * jnp.exp(running).T[:, :, None]
    ssd_out = local_out + carried + d_skip[None, :, None] * x_heads.astype(jnp.float32)
    gated_out = ssd_out.reshape(length, head_count * head_width) * jax.nn.silu(
        z_in.astype(jnp.float32)
    )
    row_squares = jnp.sum(gated_out * gated_out, axis=1)
    gated_scaled = (gated_out * norm_gain).astype(jnp.bfloat16)
    partial_value = jnp.dot(gated_scaled, out_full, preferred_element_type=jnp.float32)
    part_rows, part_squares = (
        lax.psum_scatter(partial_value, "head", scatter_dimension=0, tiled=True),
        lax.psum_scatter(row_squares, "head", scatter_dimension=0, tiled=True),
    )
    layer_sum = (
        resid.astype(jnp.float32) + part_rows * lax.rsqrt(part_squares / INNER + epsilon)[:, None]
    )
    normed = normalize_rows(layer_sum, mlp_gain)
    rows_piece = lax.all_gather(normed, "head", axis=0, tiled=True)
    gate_part = jnp.dot(rows_piece, gate_weight, preferred_element_type=jnp.float32)
    up_part = jnp.dot(rows_piece, up_weight, preferred_element_type=jnp.float32)
    hidden = (jax.nn.silu(gate_part) * up_part).astype(jnp.bfloat16)
    rows_piece = hidden
    mlp_rows = lax.psum_scatter(
        jnp.dot(rows_piece, down_full, preferred_element_type=jnp.float32),
        "head",
        scatter_dimension=0,
        tiled=True,
    )
    return (layer_sum + mlp_rows).astype(jnp.bfloat16)


def solution(mesh):
    in_specs = (
        P("seq", "head"),
        P("seq", "head"),
        P(None, "seq", None),
        P("head", "seq"),
        P("head"),
        P("head"),
        P("head"),
        P("head"),
        P("head", "seq"),
        P(("seq", "head"), None),
        P(),
        P(None, "head"),
        P(None, "head"),
        P("head", "seq"),
    )
    out_specs = P(("seq", "head"), None)
    return jax.shard_map(shards, mesh=mesh, in_specs=in_specs, out_specs=out_specs, check_vma=False)
```

profile of v0, /device:TPU:1, one launch (start us, length us, event | category | flops | bytes accessed | tf_op | source)
XLA Modules:
  0.0 857.0 jit_solution(15409193931064395106)
XLA Ops:
  14.6 30.4 %while.24 = (s32[]{:T(128)}, f32[8,64,128]{2,1,0:T(8,128)S(1)}, f32[2,256,8,64]{1,0,3,2:T(2,128)}, f32[2,8,256]{2,1,0:T(8,128)S(1)}, bf16[2,256,8,64]{1,3,2,0:T(...) while((s32[]{:T(128)}, f32[8,64,128]{2,1,0:T(8,128)S(1)}, ...), condition=%wide.region_3.4_spmd.clone, body=%wide.region_0.3_spmd.clone.sunk | while | flops 322801696 | bytes 6293764 | solution.py:50
  18.3 11.6 %dynamic_update_slice.6 = f32[2,256,8,64]{1,0,3,2:T(2,128)} dynamic-update-slice(f32[2,256,8,64]{1,0,3,2:T(2,128)} %get-tuple-element.266, f32[1,256,8,64]{1,0,3,2:T(1,128)S(1)} %copy.49, s32[]{:T(128)S(6)} %copy.54, s32[]{:T(128)} %constant.46.clone.1..sunk, s32[]{:T(128)} %constant.46.clone.1..sunk, s32[]{:T(128)} %constant.46.clone.1..sunk) | dynamic-update-slice | bytes 1048580 | tf_op jit(solution)/shard_map/while/body/jit(dynamic_update_index_in_dim)/dynamic_update_slice | solution.py:50
  33.5 11.5 %dynamic_update_slice.6 = f32[2,256,8,64]{1,0,3,2:T(2,128)} dynamic-update-slice(f32[2,256,8,64]{1,0,3,2:T(2,128)} %get-tuple-element.266, f32[1,256,8,64]{1,0,3,2:T(1,128)S(1)} %copy.49, s32[]{:T(128)S(6)} %copy.54, s32[]{:T(128)} %constant.46.clone.1..sunk, s32[]{:T(128)} %constant.46.clone.1..sunk, s32[]{:T(128)} %constant.46.clone.1..sunk) | dynamic-update-slice | bytes 1048580 | tf_op jit(solution)/shard_map/while/body/jit(dynamic_update_index_in_dim)/dynamic_update_slice | solution.py:50
  47.4 212.9 %while.23 = (s32[]{:T(128)}, f32[8,64,128]{2,1,0:T(8,128)S(1)}, f32[8]{0:T(128)S(1)}, f32[8,64,128]{2,1,0:T(8,128)S(1)}, s32[]{:T(128)}) while((s32[]{:T(128)}, f32[8,64,128]{2,1,0:T(8,128)S(1)}, f32[8]{0:T(128)S(1)}, f32[8,64,128]{2,1,0:T(8,128)S(1)}, s32[]{:T(128)}) %tuple.53), condition=%wide.region_7.8_spmd, body=%wide.region_6.7_spmd.sunk | while | flops 131074 | bytes 1835141 | solution.py:99
  47.5 10.3 %collective-permute-start = (f32[8,64,128]{2,1,0:T(8,128)S(1)}, f32[8,64,128]{2,1,0:T(8,128)S(1)}, u32[]{:S(2)}, u32[]{:S(2)}) collective-permute-start(f32[8,64,128]{2,1,0:T(8,128)S(1)} %multiply_add_fusion.3), channel_id=1, source_target_pairs={{0,16},{16,32},{32,48},{48,64},{64,80},{80,96},{96,112},{112,128},... | collective-permute-start | bytes 786440 | tf_op jit(solution)/shard_map/while/body/eval_jaxpr/ppermute | solution.py:14
  57.9 12.1 %collective-permute-done = f32[8,64,128]{2,1,0:T(8,128)S(1)} collective-permute-done((f32[8,64,128]{2,1,0:T(8,128)S(1)}, f32[8,64,128]{2,1,0:T(8,128)S(1)}, u32[]{:S(2)}, u32[]{:S(2)}) %collective-permute-start) | collective-permute-done | bytes 262176 | tf_op jit(solution)/shard_map/while/body/eval_jaxpr/ppermute | solution.py:14
  70.0 10.5 %collective-permute-start = (f32[8,64,128]{2,1,0:T(8,128)S(1)}, f32[8,64,128]{2,1,0:T(8,128)S(1)}, u32[]{:S(2)}, u32[]{:S(2)}) collective-permute-start(f32[8,64,128]{2,1,0:T(8,128)S(1)} %multiply_add_fusion.3), channel_id=1, source_target_pairs={{0,16},{16,32},{32,48},{48,64},{64,80},{80,96},{96,112},{112,128},... | collective-permute-start | bytes 786440 | tf_op jit(solution)/shard_map/while/body/eval_jaxpr/ppermute | solution.py:14
  84.5 8.4 collective-permute-start
  96.3 8.3 collective-permute-start
  108.0 8.3 collective-permute-start
  119.7 8.3 collective-permute-start
  131.4 8.3 collective-permute-start
  145.0 8.4 collective-permute-start
  153.4 6.1 collective-permute-done
  159.6 8.4 collective-permute-start
  174.0 8.4 collective-permute-start
  187.9 8.4 collective-permute-start
  196.3 6.0 collective-permute-done
  202.4 8.4 collective-permute-start
  210.8 6.0 collective-permute-done
  216.9 8.4 collective-permute-start
  225.3 6.0 collective-permute-done
  231.4 8.4 collective-permute-start
  245.9 8.4 collective-permute-start
  254.3 6.0 collective-permute-done
  264.5 7.8 fusion.41
  274.6 40.6 %all-reduce = f32[512]{0:T(512)S(1)} all-reduce(f32[512]{0:T(512)S(1)} %multiply_reduce_fusion), channel_id=3, replica_groups=mesh['seq'=16,'head'=16] {'head'}, use_global_device_ids=true, to_apply=%region_10.11.clone | all-reduce | flops 512 | bytes 4096
  315.4 157.3 %reduce-scatter.3.cloned.1.call-done = f32[32,4096]{1,0:T(8,128)} async-done(((f32[512,4096]{1,0:T(8,128)}), f32[32,4096]{1,0:T(8,128)}) %reduce-scatter.3.cloned.1.call-update) | async-done | bytes 524304 | tf_op jit(solution)/shard_map/reduce_scatter | solution.py:112
  476.8 99.1 %all-gather.6.cloned.1.call-done = bf16[512,4096]{1,0:T(8,128)(2,1)} async-done(((bf16[32,4096]{1,0:T(8,128)(2,1)}), bf16[512,4096]{1,0:T(8,128)(2,1)}) %all-gather.6.cloned.1.call-update) | async-done | bytes 4194320 | tf_op jit(solution)/shard_map/all_gather | solution.py:119
  581.7 72.2 %all-gather.8.cloned.1.call-done = bf16[512,4096]{1,0:T(8,128)(2,1)} async-done(((bf16[512,256]{1,0:T(8,128)(2,1)}), bf16[512,4096]{1,0:T(8,128)(2,1)}) %all-gather.8.cloned.1.call-update) | async-done | bytes 4194320 | tf_op jit(solution)/shard_map/all_gather | solution.py:79
  653.9 12.5 %fusion.40 = f32[512,4096]{1,0:T(8,128)} fusion(bf16[512,4096]{1,0:T(8,128)(2,1)} %all-gather.8.cloned.1.call-done, bf16[512,4096]{1,0:T(8,128)(2,1)} %all-gather.6.cloned.1.call-done, bf16[4096,512]{1,0:T(8,128)(2,1)} %param.30, f32[512,512]{1,0:T(8,128)S(1)} %fusion.52), kind=kOutput, calls=%fused_computation.61 | convolution fusion | flops 4296540160 | bytes 22020096 | tf_op jit(solution)/shard_map/dot_general | solution.py:125
  666.4 182.1 %reduce-scatter.5.cloned.1.call-done = f32[32,4096]{1,0:T(8,128)} async-done(((f32[512,4096]{1,0:T(8,128)}), f32[32,4096]{1,0:T(8,128)}) %reduce-scatter.5.cloned.1.call-update) | async-done | bytes 524304 | tf_op jit(solution)/shard_map/reduce_scatter | solution.py:124
  (105 shorter events, 76.1 us)
Async XLA Ops:
  6.5 257.9 %all-gather.4.cloned.1.call-start = ((), (), s32[]{:S(2)}) async-start(), calls=%async_computation.2 | async-start | bytes 4456448 | tf_op jit(solution)/shard_map/all_gather | solution.py:78
  7.3 465.5 %reduce-scatter.3.cloned.1.call-start = ((), (), s32[]{:S(2)}) async-start(), calls=%async_computation.3 | async-start | bytes 8912896 | tf_op jit(solution)/shard_map/reduce_scatter | solution.py:112
  45.0 215.3 %copy-start.5 = (f32[8]{0:T(128)S(1)}, f32[8]{0:T(128)}, u32[]{:S(2)}) copy-start(f32[8]{0:T(128)} %param.24) | copy-start | bytes 100
  47.4 217.1 %copy-start.2 = (bf16[512,512]{1,0:T(8,128)(2,1)S(1)}, bf16[512,512]{1,0:T(8,128)(2,1)}, u32[]{:S(2)}) copy-start(bf16[512,512]{1,0:T(8,128)(2,1)} %param.19) | copy-start | bytes 1572868
  47.4 217.1 %copy-start.3 = (f32[512]{0:T(512)S(1)}, f32[512]{0:T(512)}, u32[]{:S(2)}) copy-start(f32[512]{0:T(512)} %param.25) | copy-start | bytes 6148
  47.5 22.4 %collective-permute-start = (f32[8,64,128]{2,1,0:T(8,128)S(1)}, f32[8,64,128]{2,1,0:T(8,128)S(1)}, u32[]{:S(2)}, u32[]{:S(2)}) collective-permute-start(f32[8,64,128]{2,1,0:T(8,128)S(1)} %multiply_add_fusion.3), channel_id=1, source_target_pairs={{0,16},{16,32},{32,48},{48,64},{64,80},{80,96},{96,112},{112,128},... | collective-permute-start | bytes 786440 | tf_op jit(solution)/shard_map/while/body/eval_jaxpr/ppermute | solution.py:14
  70.0 14.4 %collective-permute-start = (f32[8,64,128]{2,1,0:T(8,128)S(1)}, f32[8,64,128]{2,1,0:T(8,128)S(1)}, u32[]{:S(2)}, u32[]{:S(2)}) collective-permute-start(f32[8,64,128]{2,1,0:T(8,128)S(1)} %multiply_add_fusion.3), channel_id=1, source_target_pairs={{0,16},{16,32},{32,48},{48,64},{64,80},{80,96},{96,112},{112,128},... | collective-permute-start | bytes 786440 | tf_op jit(solution)/shard_map/while/body/eval_jaxpr/ppermute | solution.py:14
  84.5 11.7 %collective-permute-start = (f32[8,64,128]{2,1,0:T(8,128)S(1)}, f32[8,64,128]{2,1,0:T(8,128)S(1)}, u32[]{:S(2)}, u32[]{:S(2)}) collective-permute-start(f32[8,64,128]{2,1,0:T(8,128)S(1)} %multiply_add_fusion.3), channel_id=1, source_target_pairs={{0,16},{16,32},{32,48},{48,64},{64,80},{80,96},{96,112},{112,128},... | collective-permute-start | bytes 786440 | tf_op jit(solution)/shard_map/while/body/eval_jaxpr/ppermute | solution.py:14
  96.3 11.6 %collective-permute-start = (f32[8,64,128]{2,1,0:T(8,128)S(1)}, f32[8,64,128]{2,1,0:T(8,128)S(1)}, u32[]{:S(2)}, u32[]{:S(2)}) collective-permute-start(f32[8,64,128]{2,1,0:T(8,128)S(1)} %multiply_add_fusion.3), channel_id=1, source_target_pairs={{0,16},{16,32},{32,48},{48,64},{64,80},{80,96},{96,112},{112,128},... | collective-permute-start | bytes 786440 | tf_op jit(solution)/shard_map/while/body/eval_jaxpr/ppermute | solution.py:14
  108.0 11.6 %collective-permute-start = (f32[8,64,128]{2,1,0:T(8,128)S(1)}, f32[8,64,128]{2,1,0:T(8,128)S(1)}, u32[]{:S(2)}, u32[]{:S(2)}) collective-permute-start(f32[8,64,128]{2,1,0:T(8,128)S(1)} %multiply_add_fusion.3), channel_id=1, source_target_pairs={{0,16},{16,32},{32,48},{48,64},{64,80},{80,96},{96,112},{112,128},... | collective-permute-start | bytes 786440 | tf_op jit(solution)/shard_map/while/body/eval_jaxpr/ppermute | solution.py:14
  119.7 11.6 %collective-permute-start = (f32[8,64,128]{2,1,0:T(8,128)S(1)}, f32[8,64,128]{2,1,0:T(8,128)S(1)}, u32[]{:S(2)}, u32[]{:S(2)}) collective-permute-start(f32[8,64,128]{2,1,0:T(8,128)S(1)} %multiply_add_fusion.3), channel_id=1, source_target_pairs={{0,16},{16,32},{32,48},{48,64},{64,80},{80,96},{96,112},{112,128},... | collective-permute-start | bytes 786440 | tf_op jit(solution)/shard_map/while/body/eval_jaxpr/ppermute | solution.py:14
  131.4 13.5 %collective-permute-start = (f32[8,64,128]{2,1,0:T(8,128)S(1)}, f32[8,64,128]{2,1,0:T(8,128)S(1)}, u32[]{:S(2)}, u32[]{:S(2)}) collective-permute-start(f32[8,64,128]{2,1,0:T(8,128)S(1)} %multiply_add_fusion.3), channel_id=1, source_target_pairs={{0,16},{16,32},{32,48},{48,64},{64,80},{80,96},{96,112},{112,128},... | collective-permute-start | bytes 786440 | tf_op jit(solution)/shard_map/while/body/eval_jaxpr/ppermute | solution.py:14
  145.0 14.5 %collective-permute-start = (f32[8,64,128]{2,1,0:T(8,128)S(1)}, f32[8,64,128]{2,1,0:T(8,128)S(1)}, u32[]{:S(2)}, u32[]{:S(2)}) collective-permute-start(f32[8,64,128]{2,1,0:T(8,128)S(1)} %multiply_add_fusion.3), channel_id=1, source_target_pairs={{0,16},{16,32},{32,48},{48,64},{64,80},{80,96},{96,112},{112,128},... | collective-permute-start | bytes 786440 | tf_op jit(solution)/shard_map/while/body/eval_jaxpr/ppermute | solution.py:14
  159.6 14.3 %collective-permute-start = (f32[8,64,128]{2,1,0:T(8,128)S(1)}, f32[8,64,128]{2,1,0:T(8,128)S(1)}, u32[]{:S(2)}, u32[]{:S(2)}) collective-permute-start(f32[8,64,128]{2,1,0:T(8,128)S(1)} %multiply_add_fusion.3), channel_id=1, source_target_pairs={{0,16},{16,32},{32,48},{48,64},{64,80},{80,96},{96,112},{112,128},... | collective-permute-start | bytes 786440 | tf_op jit(solution)/shard_map/while/body/eval_jaxpr/ppermute | solution.py:14
  174.0 13.8 %collective-permute-start = (f32[8,64,128]{2,1,0:T(8,128)S(1)}, f32[8,64,128]{2,1,0:T(8,128)S(1)}, u32[]{:S(2)}, u32[]{:S(2)}) collective-permute-start(f32[8,64,128]{2,1,0:T(8,128)S(1)} %multiply_add_fusion.3), channel_id=1, source_target_pairs={{0,16},{16,32},{32,48},{48,64},{64,80},{80,96},{96,112},{112,128},... | collective-permute-start | bytes 786440 | tf_op jit(solution)/shard_map/while/body/eval_jaxpr/ppermute | solution.py:14
  187.9 14.4 %collective-permute-start = (f32[8,64,128]{2,1,0:T(8,128)S(1)}, f32[8,64,128]{2,1,0:T(8,128)S(1)}, u32[]{:S(2)}, u32[]{:S(2)}) collective-permute-start(f32[8,64,128]{2,1,0:T(8,128)S(1)} %multiply_add_fusion.3), channel_id=1, source_target_pairs={{0,16},{16,32},{32,48},{48,64},{64,80},{80,96},{96,112},{112,128},... | collective-permute-start | bytes 786440 | tf_op jit(solution)/shard_map/while/body/eval_jaxpr/ppermute | solution.py:14
  202.4 14.4 %collective-permute-start = (f32[8,64,128]{2,1,0:T(8,128)S(1)}, f32[8,64,128]{2,1,0:T(8,128)S(1)}, u32[]{:S(2)}, u32[]{:S(2)}) collective-permute-start(f32[8,64,128]{2,1,0:T(8,128)S(1)} %multiply_add_fusion.3), channel_id=1, source_target_pairs={{0,16},{16,32},{32,48},{48,64},{64,80},{80,96},{96,112},{112,128},... | collective-permute-start | bytes 786440 | tf_op jit(solution)/shard_map/while/body/eval_jaxpr/ppermute | solution.py:14
  216.9 14.4 %collective-permute-start = (f32[8,64,128]{2,1,0:T(8,128)S(1)}, f32[8,64,128]{2,1,0:T(8,128)S(1)}, u32[]{:S(2)}, u32[]{:S(2)}) collective-permute-start(f32[8,64,128]{2,1,0:T(8,128)S(1)} %multiply_add_fusion.3), channel_id=1, source_target_pairs={{0,16},{16,32},{32,48},{48,64},{64,80},{80,96},{96,112},{112,128},... | collective-permute-start | bytes 786440 | tf_op jit(solution)/shard_map/while/body/eval_jaxpr/ppermute | solution.py:14
  231.4 14.4 %collective-permute-start = (f32[8,64,128]{2,1,0:T(8,128)S(1)}, f32[8,64,128]{2,1,0:T(8,128)S(1)}, u32[]{:S(2)}, u32[]{:S(2)}) collective-permute-start(f32[8,64,128]{2,1,0:T(8,128)S(1)} %multiply_add_fusion.3), channel_id=1, source_target_pairs={{0,16},{16,32},{32,48},{48,64},{64,80},{80,96},{96,112},{112,128},... | collective-permute-start | bytes 786440 | tf_op jit(solution)/shard_map/while/body/eval_jaxpr/ppermute | solution.py:14
  245.9 14.4 %collective-permute-start = (f32[8,64,128]{2,1,0:T(8,128)S(1)}, f32[8,64,128]{2,1,0:T(8,128)S(1)}, u32[]{:S(2)}, u32[]{:S(2)}) collective-permute-start(f32[8,64,128]{2,1,0:T(8,128)S(1)} %multiply_add_fusion.3), channel_id=1, source_target_pairs={{0,16},{16,32},{32,48},{48,64},{64,80},{80,96},{96,112},{112,128},... | collective-permute-start | bytes 786440 | tf_op jit(solution)/shard_map/while/body/eval_jaxpr/ppermute | solution.py:14
  272.3 0.7 copy-start.6
  272.3 200.4 %copy-start.1 = (bf16[32,4096]{1,0:T(8,128)(2,1)S(1)}, bf16[32,4096]{1,0:T(8,128)(2,1)}, u32[]{:S(2)}) copy-start(bf16[32,4096]{1,0:T(8,128)(2,1)} %param.27) | copy-start | bytes 786436
  272.3 201.7 %copy-start.4 = (f32[4096]{0:T(1024)S(1)}, f32[4096]{0:T(1024)}, u32[]{:S(2)}) copy-start(f32[4096]{0:T(1024)} %param.28) | copy-start | bytes 49156
  272.3 303.6 %all-gather.6.cloned.1.call-start = ((), (), s32[]{:S(2)}) async-start(), calls=%async_computation.4 | async-start | bytes 4456448 | tf_op jit(solution)/shard_map/all_gather | solution.py:119
  476.0 177.9 %all-gather.8.cloned.1.call-start = ((), (), s32[]{:S(2)}) async-start(), calls=%async_computation.5 | async-start | bytes 4456448 | tf_op jit(solution)/shard_map/all_gather | solution.py:79
  476.6 372.0 %reduce-scatter.5.cloned.1.call-start = ((), (), s32[]{:S(2)}) async-start(), calls=%async_computation.6 | async-start | bytes 8912896 | tf_op jit(solution)/shard_map/reduce_scatter | solution.py:124
  666.4 182.1 %copy-start = (f32[32,4096]{1,0:T(8,128)S(1)}, f32[32,4096]{1,0:T(8,128)}, u32[]{:S(2)}) copy-start(f32[32,4096]{1,0:T(8,128)} %reduce-scatter.3.cloned.1.call-done) | copy-start | bytes 1572868
Sparse Core Ops, SparseCore 0:
  9.9 89.6 all-gather.3
  272.5 200.2 reduce-scatter.2
  476.1 99.7 all-gather.5
  578.3 75.5 all-gather.7
  666.5 181.9 reduce-scatter.4
where the time goes:
time: 859 us; the launch traced here: 857 us
  waiting for transfers between devices  594 us (69%)
  starting transfers between devices  130 us (15%)
  blocking collectives  40.6 us (5%)
  local copies, waits for them, and re-layouts  34.6 us (4%)
  matrix products  32.4 us (4%)
  between operations  13.9 us (2%)
  other arithmetic  11.3 us (1%)
    reduce_scatter x1, waiting for transfers between devices, shards(): lax.psum_scatter(jnp.dot(rows_piece, down_full, preferred_element_type=jn...  182 us
    reduce_scatter x1, waiting for transfers between devices, shards(): lax.psum_scatter(partial_value, 'head', scatter_dimension=0, tiled=True)  157 us
    ppermute x15, starting transfers between devices, passed_along(): lax.ppermute(value, axis, [(source, source + steps) for source in range(i...  130 us
    all_gather x1, waiting for transfers between devices, shards(): rows_piece = lax.all_gather(normed, 'head', axis=0, tiled=True)  99.1 us
    ppermute x15, waiting for transfers between devices, passed_along(): lax.ppermute(value, axis, [(source, source + steps) for source in range(i...  81.7 us
    all_gather x1, waiting for transfers between devices, shards(): lax.all_gather(down_weight, 'seq', axis=1, tiled=True)  72.2 us
    unnamed x1, blocking collectives  40.6 us
    dynamic_update_slice x4, local copies, waits for them, and re-layouts, block_scan(): lax.scan(advance, start_state, (x_blocks, b_blocks, c_blocks, d_blocks, a...  24.2 us
  transfers between devices with their start and end apart: 20, of which 19 were waited for; matrix products, arithmetic and copies ran while one was open for 6% of the time, Pallas kernels for 0%

commit v1 on v0

--- a/solution.py
+++ b/solution.py
@@ -116,7 +116,8 @@
         resid.astype(jnp.float32) + part_rows * lax.rsqrt(part_squares / INNER + epsilon)[:, None]
     )
     normed = normalize_rows(layer_sum, mlp_gain)
-    rows_piece = lax.all_gather(normed, "head", axis=0, tiled=True)
+    sent = jnp.stack([normed] * lax.axis_size("head"))
+    rows_piece = jnp.concatenate(lax.all_to_all(sent, "head", 0, 0), axis=0)
     gate_part = jnp.dot(rows_piece, gate_weight, preferred_element_type=jnp.float32)
     up_part = jnp.dot(rows_piece, up_weight, preferred_element_type=jnp.float32)
     hidden = (jax.nn.silu(gate_part) * up_part).astype(jnp.bfloat16)

time: 859 us -> 822 us (0.957)
  waiting for transfers between devices: 594 us -> 548 us
    all_to_all x0 -> x1, waiting for transfers between devices: none -> 123 us  [shards(): rows_piece = jnp.concatenate(lax.all_to_all(sent, 'head', 0, 0), axis=0)]
    all_gather x1 -> x0, waiting for transfers between devices: 99.1 us -> none  [shards(): rows_piece = lax.all_gather(normed, 'head', axis=0, tiled=True)]
    all_gather x1, waiting for transfers between devices: 72.2 us -> 0.02 us  [shards(): lax.all_gather(down_weight, 'seq', axis=1, tiled=True)]
  transfers between devices with their start and end apart: 20 -> 20, of which waited for: 19 -> 18; matrix products, arithmetic and copies ran while one was open for 6% -> 6% of each run, Pallas kernels for 0% -> 0%
where the time goes in v1:
time: 822 us; the launch traced here: 819 us
  waiting for transfers between devices  548 us (67%)
  starting transfers between devices  136 us (17%)
  blocking collectives  40.9 us (5%)
  local copies, waits for them, and re-layouts  37.1 us (5%)
  matrix products  32.4 us (4%)
  between operations  13.9 us (2%)
  other arithmetic  10.6 us (1%)
    reduce_scatter x1, waiting for transfers between devices, shards(): lax.psum_scatter(jnp.dot(rows_piece, down_full, preferred_element_type=jn...  184 us
    reduce_scatter x1, waiting for transfers between devices, shards(): lax.psum_scatter(partial_value, 'head', scatter_dimension=0, tiled=True)  157 us
    ppermute x15, starting transfers between devices, passed_along(): lax.ppermute(value, axis, [(source, source + steps) for source in range(i...  130 us
    all_to_all x1, waiting for transfers between devices, shards(): rows_piece = jnp.concatenate(lax.all_to_all(sent, 'head', 0, 0), axis=0)  123 us
    ppermute x15, waiting for transfers between devices, passed_along(): lax.ppermute(value, axis, [(source, source + steps) for source in range(i...  81.7 us
    unnamed x1, blocking collectives  40.9 us
    dynamic_update_slice x4, local copies, waits for them, and re-layouts, block_scan(): lax.scan(advance, start_state, (x_blocks, b_blocks, c_blocks, d_blocks, a...  24.2 us
  transfers between devices with their start and end apart: 20, of which 18 were waited for; matrix products, arithmetic and copies ran while one was open for 6% of the time, Pallas kernels for 0%

profile of v1, /device:TPU:1, one launch (start us, length us, event | category | flops | bytes accessed | tf_op | source)
XLA Modules:
  0.0 819.3 jit_solution(8749871022875343573)
XLA Ops:
  14.6 30.3 %while.24 = (s32[]{:T(128)}, f32[8,64,128]{2,1,0:T(8,128)S(1)}, f32[2,256,8,64]{1,0,3,2:T(2,128)}, f32[2,8,256]{2,1,0:T(8,128)S(1)}, bf16[2,256,8,64]{1,3,2,0:T(...) while((s32[]{:T(128)}, f32[8,64,128]{2,1,0:T(8,128)S(1)}, ...), condition=%wide.region_3.4_spmd.clone, body=%wide.region_0.3_spmd.clone.sunk | while | flops 322801696 | bytes 6293764 | solution.py:50
  18.3 11.6 %dynamic_update_slice.6 = f32[2,256,8,64]{1,0,3,2:T(2,128)} dynamic-update-slice(f32[2,256,8,64]{1,0,3,2:T(2,128)} %get-tuple-element.266, f32[1,256,8,64]{1,0,3,2:T(1,128)S(1)} %copy.49, s32[]{:T(128)S(6)} %copy.54, s32[]{:T(128)} %constant.46.clone.1..sunk, s32[]{:T(128)} %constant.46.clone.1..sunk, s32[]{:T(128)} %constant.46.clone.1..sunk) | dynamic-update-slice | bytes 1048580 | tf_op jit(solution)/shard_map/while/body/jit(dynamic_update_index_in_dim)/dynamic_update_slice | solution.py:50
  33.4 11.5 %dynamic_update_slice.6 = f32[2,256,8,64]{1,0,3,2:T(2,128)} dynamic-update-slice(f32[2,256,8,64]{1,0,3,2:T(2,128)} %get-tuple-element.266, f32[1,256,8,64]{1,0,3,2:T(1,128)S(1)} %copy.49, s32[]{:T(128)S(6)} %copy.54, s32[]{:T(128)} %constant.46.clone.1..sunk, s32[]{:T(128)} %constant.46.clone.1..sunk, s32[]{:T(128)} %constant.46.clone.1..sunk) | dynamic-update-slice | bytes 1048580 | tf_op jit(solution)/shard_map/while/body/jit(dynamic_update_index_in_dim)/dynamic_update_slice | solution.py:50
  47.4 212.8 %while.23 = (s32[]{:T(128)}, f32[8,64,128]{2,1,0:T(8,128)S(1)}, f32[8]{0:T(128)S(1)}, f32[8,64,128]{2,1,0:T(8,128)S(1)}, s32[]{:T(128)}) while((s32[]{:T(128)}, f32[8,64,128]{2,1,0:T(8,128)S(1)}, f32[8]{0:T(128)S(1)}, f32[8,64,128]{2,1,0:T(8,128)S(1)}, s32[]{:T(128)}) %tuple.53), condition=%wide.region_7.8_spmd, body=%wide.region_6.7_spmd.sunk | while | flops 131074 | bytes 1835141 | solution.py:99
  47.5 10.3 %collective-permute-start = (f32[8,64,128]{2,1,0:T(8,128)S(1)}, f32[8,64,128]{2,1,0:T(8,128)S(1)}, u32[]{:S(2)}, u32[]{:S(2)}) collective-permute-start(f32[8,64,128]{2,1,0:T(8,128)S(1)} %multiply_add_fusion.3), channel_id=1, source_target_pairs={{0,16},{16,32},{32,48},{48,64},{64,80},{80,96},{96,112},{112,128},... | collective-permute-start | bytes 786440 | tf_op jit(solution)/shard_map/while/body/eval_jaxpr/ppermute | solution.py:14
  57.8 12.1 %collective-permute-done = f32[8,64,128]{2,1,0:T(8,128)S(1)} collective-permute-done((f32[8,64,128]{2,1,0:T(8,128)S(1)}, f32[8,64,128]{2,1,0:T(8,128)S(1)}, u32[]{:S(2)}, u32[]{:S(2)}) %collective-permute-start) | collective-permute-done | bytes 262176 | tf_op jit(solution)/shard_map/while/body/eval_jaxpr/ppermute | solution.py:14
  70.0 10.5 %collective-permute-start = (f32[8,64,128]{2,1,0:T(8,128)S(1)}, f32[8,64,128]{2,1,0:T(8,128)S(1)}, u32[]{:S(2)}, u32[]{:S(2)}) collective-permute-start(f32[8,64,128]{2,1,0:T(8,128)S(1)} %multiply_add_fusion.3), channel_id=1, source_target_pairs={{0,16},{16,32},{32,48},{48,64},{64,80},{80,96},{96,112},{112,128},... | collective-permute-start | bytes 786440 | tf_op jit(solution)/shard_map/while/body/eval_jaxpr/ppermute | solution.py:14
  84.5 8.4 %collective-permute-start = (f32[8,64,128]{2,1,0:T(8,128)S(1)}, f32[8,64,128]{2,1,0:T(8,128)S(1)}, u32[]{:S(2)}, u32[]{:S(2)}) collective-permute-start(f32[8,64,128]{2,1,0:T(8,128)S(1)} %multiply_add_fusion.3), channel_id=1, source_target_pairs={{0,16},{16,32},{32,48},{48,64},{64,80},{80,96},{96,112},{112,128},... | collective-permute-start | bytes 786440 | tf_op jit(solution)/shard_map/while/body/eval_jaxpr/ppermute | solution.py:14
  96.2 8.3 %collective-permute-start = (f32[8,64,128]{2,1,0:T(8,128)S(1)}, f32[8,64,128]{2,1,0:T(8,128)S(1)}, u32[]{:S(2)}, u32[]{:S(2)}) collective-permute-start(f32[8,64,128]{2,1,0:T(8,128)S(1)} %multiply_add_fusion.3), channel_id=1, source_target_pairs={{0,16},{16,32},{32,48},{48,64},{64,80},{80,96},{96,112},{112,128},... | collective-permute-start | bytes 786440 | tf_op jit(solution)/shard_map/while/body/eval_jaxpr/ppermute | solution.py:14
  107.9 8.3 %collective-permute-start = (f32[8,64,128]{2,1,0:T(8,128)S(1)}, f32[8,64,128]{2,1,0:T(8,128)S(1)}, u32[]{:S(2)}, u32[]{:S(2)}) collective-permute-start(f32[8,64,128]{2,1,0:T(8,128)S(1)} %multiply_add_fusion.3), channel_id=1, source_target_pairs={{0,16},{16,32},{32,48},{48,64},{64,80},{80,96},{96,112},{112,128},... | collective-permute-start | bytes 786440 | tf_op jit(solution)/shard_map/while/body/eval_jaxpr/ppermute | solution.py:14
  119.6 8.3 %collective-permute-start = (f32[8,64,128]{2,1,0:T(8,128)S(1)}, f32[8,64,128]{2,1,0:T(8,128)S(1)}, u32[]{:S(2)}, u32[]{:S(2)}) collective-permute-start(f32[8,64,128]{2,1,0:T(8,128)S(1)} %multiply_add_fusion.3), channel_id=1, source_target_pairs={{0,16},{16,32},{32,48},{48,64},{64,80},{80,96},{96,112},{112,128},... | collective-permute-start | bytes 786440 | tf_op jit(solution)/shard_map/while/body/eval_jaxpr/ppermute | solution.py:14
  131.4 8.3 %collective-permute-start = (f32[8,64,128]{2,1,0:T(8,128)S(1)}, f32[8,64,128]{2,1,0:T(8,128)S(1)}, u32[]{:S(2)}, u32[]{:S(2)}) collective-permute-start(f32[8,64,128]{2,1,0:T(8,128)S(1)} %multiply_add_fusion.3), channel_id=1, source_target_pairs={{0,16},{16,32},{32,48},{48,64},{64,80},{80,96},{96,112},{112,128},... | collective-permute-start | bytes 786440 | tf_op jit(solution)/shard_map/while/body/eval_jaxpr/ppermute | solution.py:14
  144.9 8.4 %collective-permute-start = (f32[8,64,128]{2,1,0:T(8,128)S(1)}, f32[8,64,128]{2,1,0:T(8,128)S(1)}, u32[]{:S(2)}, u32[]{:S(2)}) collective-permute-start(f32[8,64,128]{2,1,0:T(8,128)S(1)} %multiply_add_fusion.3), channel_id=1, source_target_pairs={{0,16},{16,32},{32,48},{48,64},{64,80},{80,96},{96,112},{112,128},... | collective-permute-start | bytes 786440 | tf_op jit(solution)/shard_map/while/body/eval_jaxpr/ppermute | solution.py:14
  153.4 6.1 collective-permute-done
  159.5 8.4 %collective-permute-start = (f32[8,64,128]{2,1,0:T(8,128)S(1)}, f32[8,64,128]{2,1,0:T(8,128)S(1)}, u32[]{:S(2)}, u32[]{:S(2)}) collective-permute-start(f32[8,64,128]{2,1,0:T(8,128)S(1)} %multiply_add_fusion.3), channel_id=1, source_target_pairs={{0,16},{16,32},{32,48},{48,64},{64,80},{80,96},{96,112},{112,128},... | collective-permute-start | bytes 786440 | tf_op jit(solution)/shard_map/while/body/eval_jaxpr/ppermute | solution.py:14
  173.9 8.4 %collective-permute-start = (f32[8,64,128]{2,1,0:T(8,128)S(1)}, f32[8,64,128]{2,1,0:T(8,128)S(1)}, u32[]{:S(2)}, u32[]{:S(2)}) collective-permute-start(f32[8,64,128]{2,1,0:T(8,128)S(1)} %multiply_add_fusion.3), channel_id=1, source_target_pairs={{0,16},{16,32},{32,48},{48,64},{64,80},{80,96},{96,112},{112,128},... | collective-permute-start | bytes 786440 | tf_op jit(solution)/shard_map/while/body/eval_jaxpr/ppermute | solution.py:14
  187.8 8.4 %collective-permute-start = (f32[8,64,128]{2,1,0:T(8,128)S(1)}, f32[8,64,128]{2,1,0:T(8,128)S(1)}, u32[]{:S(2)}, u32[]{:S(2)}) collective-permute-start(f32[8,64,128]{2,1,0:T(8,128)S(1)} %multiply_add_fusion.3), channel_id=1, source_target_pairs={{0,16},{16,32},{32,48},{48,64},{64,80},{80,96},{96,112},{112,128},... | collective-permute-start | bytes 786440 | tf_op jit(solution)/shard_map/while/body/eval_jaxpr/ppermute | solution.py:14
  196.2 6.0 collective-permute-done
  202.3 8.4 %collective-permute-start = (f32[8,64,128]{2,1,0:T(8,128)S(1)}, f32[8,64,128]{2,1,0:T(8,128)S(1)}, u32[]{:S(2)}, u32[]{:S(2)}) collective-permute-start(f32[8,64,128]{2,1,0:T(8,128)S(1)} %multiply_add_fusion.3), channel_id=1, source_target_pairs={{0,16},{16,32},{32,48},{48,64},{64,80},{80,96},{96,112},{112,128},... | collective-permute-start | bytes 786440 | tf_op jit(solution)/shard_map/while/body/eval_jaxpr/ppermute | solution.py:14
  216.8 8.4 %collective-permute-start = (f32[8,64,128]{2,1,0:T(8,128)S(1)}, f32[8,64,128]{2,1,0:T(8,128)S(1)}, u32[]{:S(2)}, u32[]{:S(2)}) collective-permute-start(f32[8,64,128]{2,1,0:T(8,128)S(1)} %multiply_add_fusion.3), channel_id=1, source_target_pairs={{0,16},{16,32},{32,48},{48,64},{64,80},{80,96},{96,112},{112,128},... | collective-permute-start | bytes 786440 | tf_op jit(solution)/shard_map/while/body/eval_jaxpr/ppermute | solution.py:14
  225.2 6.0 collective-permute-done
  231.3 8.4 %collective-permute-start = (f32[8,64,128]{2,1,0:T(8,128)S(1)}, f32[8,64,128]{2,1,0:T(8,128)S(1)}, u32[]{:S(2)}, u32[]{:S(2)}) collective-permute-start(f32[8,64,128]{2,1,0:T(8,128)S(1)} %multiply_add_fusion.3), channel_id=1, source_target_pairs={{0,16},{16,32},{32,48},{48,64},{64,80},{80,96},{96,112},{112,128},... | collective-permute-start | bytes 786440 | tf_op jit(solution)/shard_map/while/body/eval_jaxpr/ppermute | solution.py:14
  239.7 6.0 collective-permute-done
  245.8 8.4 %collective-permute-start = (f32[8,64,128]{2,1,0:T(8,128)S(1)}, f32[8,64,128]{2,1,0:T(8,128)S(1)}, u32[]{:S(2)}, u32[]{:S(2)}) collective-permute-start(f32[8,64,128]{2,1,0:T(8,128)S(1)} %multiply_add_fusion.3), channel_id=1, source_target_pairs={{0,16},{16,32},{32,48},{48,64},{64,80},{80,96},{96,112},{112,128},... | collective-permute-start | bytes 786440 | tf_op jit(solution)/shard_map/while/body/eval_jaxpr/ppermute | solution.py:14
  254.2 6.0 collective-permute-done
  264.4 7.8 fusion.41
  274.6 40.9 %all-reduce = f32[512]{0:T(512)S(1)} all-reduce(f32[512]{0:T(512)S(1)} %multiply_reduce_fusion), channel_id=3, replica_groups=mesh['seq'=16,'head'=16] {'head'}, use_global_device_ids=true, to_apply=%region_10.11.clone | all-reduce | flops 512 | bytes 4096
  315.5 157.2 %reduce-scatter.3.cloned.1.call-done = f32[32,4096]{1,0:T(8,128)} async-done(((f32[512,4096]{1,0:T(8,128)}), f32[32,4096]{1,0:T(8,128)}) %reduce-scatter.3.cloned.1.call-update) | async-done | bytes 524304 | tf_op jit(solution)/shard_map/reduce_scatter | solution.py:112
  477.7 6.4 all-to-all-start
  485.1 123.4 %all-to-all-done = bf16[16,32,4096]{2,1,0:T(8,128)(2,1)} async-done(((bf16[16,32,4096]{2,1,0:T(8,128)(2,1)}), bf16[16,32,4096]{2,1,0:T(8,128)(2,1)}, u32[]{:S(2)}, u32[]{:S(2)}) %all-to-all-start) | async-done | bytes 4194336 | tf_op jit(solution)/shard_map/all_to_all | solution.py:120
  614.4 12.5 %fusion.40 = f32[512,4096]{1,0:T(8,128)} fusion(bf16[512,4096]{1,0:T(8,128)(2,1)} %all-gather.5.cloned.1.call-done, bf16[512,4096]{1,0:T(8,128)(2,1)} %bitcast.14, bf16[4096,512]{1,0:T(8,128)(2,1)} %param.30, f32[512,512]{1,0:T(8,128)S(1)} %fusion.52), kind=kOutput, calls=%fused_computation.61 | convolution fusion | flops 4296540160 | bytes 22020096 | tf_op jit(solution)/shard_map/dot_general | solution.py:126
  626.9 183.9 %reduce-scatter.5.cloned.1.call-done = f32[32,4096]{1,0:T(8,128)} async-done(((f32[512,4096]{1,0:T(8,128)}), f32[32,4096]{1,0:T(8,128)}) %reduce-scatter.5.cloned.1.call-update) | async-done | bytes 524304 | tf_op jit(solution)/shard_map/reduce_scatter | solution.py:125
  (105 shorter events, 77.9 us)
Async XLA Ops:
  6.5 257.8 %all-gather.3.cloned.1.call-start = ((), (), s32[]{:S(2)}) async-start(), calls=%async_computation.3 | async-start | bytes 4456448 | tf_op jit(solution)/shard_map/all_gather | solution.py:78
  7.3 465.5 %reduce-scatter.3.cloned.1.call-start = ((), (), s32[]{:S(2)}) async-start(), calls=%async_computation.4 | async-start | bytes 8912896 | tf_op jit(solution)/shard_map/reduce_scatter | solution.py:112
  45.0 215.2 %copy-start.5 = (f32[8]{0:T(128)S(1)}, f32[8]{0:T(128)}, u32[]{:S(2)}) copy-start(f32[8]{0:T(128)} %param.24) | copy-start | bytes 100
  47.4 217.0 %copy-start.2 = (bf16[512,512]{1,0:T(8,128)(2,1)S(1)}, bf16[512,512]{1,0:T(8,128)(2,1)}, u32[]{:S(2)}) copy-start(bf16[512,512]{1,0:T(8,128)(2,1)} %param.19) | copy-start | bytes 1572868
  47.4 217.0 %copy-start.3 = (f32[512]{0:T(512)S(1)}, f32[512]{0:T(512)}, u32[]{:S(2)}) copy-start(f32[512]{0:T(512)} %param.25) | copy-start | bytes 6148
  47.5 22.4 %collective-permute-start = (f32[8,64,128]{2,1,0:T(8,128)S(1)}, f32[8,64,128]{2,1,0:T(8,128)S(1)}, u32[]{:S(2)}, u32[]{:S(2)}) collective-permute-start(f32[8,64,128]{2,1,0:T(8,128)S(1)} %multiply_add_fusion.3), channel_id=1, source_target_pairs={{0,16},{16,32},{32,48},{48,64},{64,80},{80,96},{96,112},{112,128},... | collective-permute-start | bytes 786440 | tf_op jit(solution)/shard_map/while/body/eval_jaxpr/ppermute | solution.py:14
  70.0 14.4 %collective-permute-start = (f32[8,64,128]{2,1,0:T(8,128)S(1)}, f32[8,64,128]{2,1,0:T(8,128)S(1)}, u32[]{:S(2)}, u32[]{:S(2)}) collective-permute-start(f32[8,64,128]{2,1,0:T(8,128)S(1)} %multiply_add_fusion.3), channel_id=1, source_target_pairs={{0,16},{16,32},{32,48},{48,64},{64,80},{80,96},{96,112},{112,128},... | collective-permute-start | bytes 786440 | tf_op jit(solution)/shard_map/while/body/eval_jaxpr/ppermute | solution.py:14
  84.5 11.7 %collective-permute-start = (f32[8,64,128]{2,1,0:T(8,128)S(1)}, f32[8,64,128]{2,1,0:T(8,128)S(1)}, u32[]{:S(2)}, u32[]{:S(2)}) collective-permute-start(f32[8,64,128]{2,1,0:T(8,128)S(1)} %multiply_add_fusion.3), channel_id=1, source_target_pairs={{0,16},{16,32},{32,48},{48,64},{64,80},{80,96},{96,112},{112,128},... | collective-permute-start | bytes 786440 | tf_op jit(solution)/shard_map/while/body/eval_jaxpr/ppermute | solution.py:14
  96.2 11.6 %collective-permute-start = (f32[8,64,128]{2,1,0:T(8,128)S(1)}, f32[8,64,128]{2,1,0:T(8,128)S(1)}, u32[]{:S(2)}, u32[]{:S(2)}) collective-permute-start(f32[8,64,128]{2,1,0:T(8,128)S(1)} %multiply_add_fusion.3), channel_id=1, source_target_pairs={{0,16},{16,32},{32,48},{48,64},{64,80},{80,96},{96,112},{112,128},... | collective-permute-start | bytes 786440 | tf_op jit(solution)/shard_map/while/body/eval_jaxpr/ppermute | solution.py:14
  107.9 11.6 %collective-permute-start = (f32[8,64,128]{2,1,0:T(8,128)S(1)}, f32[8,64,128]{2,1,0:T(8,128)S(1)}, u32[]{:S(2)}, u32[]{:S(2)}) collective-permute-start(f32[8,64,128]{2,1,0:T(8,128)S(1)} %multiply_add_fusion.3), channel_id=1, source_target_pairs={{0,16},{16,32},{32,48},{48,64},{64,80},{80,96},{96,112},{112,128},... | collective-permute-start | bytes 786440 | tf_op jit(solution)/shard_map/while/body/eval_jaxpr/ppermute | solution.py:14
  119.6 11.6 %collective-permute-start = (f32[8,64,128]{2,1,0:T(8,128)S(1)}, f32[8,64,128]{2,1,0:T(8,128)S(1)}, u32[]{:S(2)}, u32[]{:S(2)}) collective-permute-start(f32[8,64,128]{2,1,0:T(8,128)S(1)} %multiply_add_fusion.3), channel_id=1, source_target_pairs={{0,16},{16,32},{32,48},{48,64},{64,80},{80,96},{96,112},{112,128},... | collective-permute-start | bytes 786440 | tf_op jit(solution)/shard_map/while/body/eval_jaxpr/ppermute | solution.py:14
  131.4 13.5 %collective-permute-start = (f32[8,64,128]{2,1,0:T(8,128)S(1)}, f32[8,64,128]{2,1,0:T(8,128)S(1)}, u32[]{:S(2)}, u32[]{:S(2)}) collective-permute-start(f32[8,64,128]{2,1,0:T(8,128)S(1)} %multiply_add_fusion.3), channel_id=1, source_target_pairs={{0,16},{16,32},{32,48},{48,64},{64,80},{80,96},{96,112},{112,128},... | collective-permute-start | bytes 786440 | tf_op jit(solution)/shard_map/while/body/eval_jaxpr/ppermute | solution.py:14
  144.9 14.5 %collective-permute-start = (f32[8,64,128]{2,1,0:T(8,128)S(1)}, f32[8,64,128]{2,1,0:T(8,128)S(1)}, u32[]{:S(2)}, u32[]{:S(2)}) collective-permute-start(f32[8,64,128]{2,1,0:T(8,128)S(1)} %multiply_add_fusion.3), channel_id=1, source_target_pairs={{0,16},{16,32},{32,48},{48,64},{64,80},{80,96},{96,112},{112,128},... | collective-permute-start | bytes 786440 | tf_op jit(solution)/shard_map/while/body/eval_jaxpr/ppermute | solution.py:14
  159.5 14.3 %collective-permute-start = (f32[8,64,128]{2,1,0:T(8,128)S(1)}, f32[8,64,128]{2,1,0:T(8,128)S(1)}, u32[]{:S(2)}, u32[]{:S(2)}) collective-permute-start(f32[8,64,128]{2,1,0:T(8,128)S(1)} %multiply_add_fusion.3), channel_id=1, source_target_pairs={{0,16},{16,32},{32,48},{48,64},{64,80},{80,96},{96,112},{112,128},... | collective-permute-start | bytes 786440 | tf_op jit(solution)/shard_map/while/body/eval_jaxpr/ppermute | solution.py:14
  173.9 13.8 %collective-permute-start = (f32[8,64,128]{2,1,0:T(8,128)S(1)}, f32[8,64,128]{2,1,0:T(8,128)S(1)}, u32[]{:S(2)}, u32[]{:S(2)}) collective-permute-start(f32[8,64,128]{2,1,0:T(8,128)S(1)} %multiply_add_fusion.3), channel_id=1, source_target_pairs={{0,16},{16,32},{32,48},{48,64},{64,80},{80,96},{96,112},{112,128},... | collective-permute-start | bytes 786440 | tf_op jit(solution)/shard_map/while/body/eval_jaxpr/ppermute | solution.py:14
  187.8 14.4 %collective-permute-start = (f32[8,64,128]{2,1,0:T(8,128)S(1)}, f32[8,64,128]{2,1,0:T(8,128)S(1)}, u32[]{:S(2)}, u32[]{:S(2)}) collective-permute-start(f32[8,64,128]{2,1,0:T(8,128)S(1)} %multiply_add_fusion.3), channel_id=1, source_target_pairs={{0,16},{16,32},{32,48},{48,64},{64,80},{80,96},{96,112},{112,128},... | collective-permute-start | bytes 786440 | tf_op jit(solution)/shard_map/while/body/eval_jaxpr/ppermute | solution.py:14
  202.3 14.4 %collective-permute-start = (f32[8,64,128]{2,1,0:T(8,128)S(1)}, f32[8,64,128]{2,1,0:T(8,128)S(1)}, u32[]{:S(2)}, u32[]{:S(2)}) collective-permute-start(f32[8,64,128]{2,1,0:T(8,128)S(1)} %multiply_add_fusion.3), channel_id=1, source_target_pairs={{0,16},{16,32},{32,48},{48,64},{64,80},{80,96},{96,112},{112,128},... | collective-permute-start | bytes 786440 | tf_op jit(solution)/shard_map/while/body/eval_jaxpr/ppermute | solution.py:14
  216.8 14.4 %collective-permute-start = (f32[8,64,128]{2,1,0:T(8,128)S(1)}, f32[8,64,128]{2,1,0:T(8,128)S(1)}, u32[]{:S(2)}, u32[]{:S(2)}) collective-permute-start(f32[8,64,128]{2,1,0:T(8,128)S(1)} %multiply_add_fusion.3), channel_id=1, source_target_pairs={{0,16},{16,32},{32,48},{48,64},{64,80},{80,96},{96,112},{112,128},... | collective-permute-start | bytes 786440 | tf_op jit(solution)/shard_map/while/body/eval_jaxpr/ppermute | solution.py:14
  231.3 14.4 %collective-permute-start = (f32[8,64,128]{2,1,0:T(8,128)S(1)}, f32[8,64,128]{2,1,0:T(8,128)S(1)}, u32[]{:S(2)}, u32[]{:S(2)}) collective-permute-start(f32[8,64,128]{2,1,0:T(8,128)S(1)} %multiply_add_fusion.3), channel_id=1, source_target_pairs={{0,16},{16,32},{32,48},{48,64},{64,80},{80,96},{96,112},{112,128},... | collective-permute-start | bytes 786440 | tf_op jit(solution)/shard_map/while/body/eval_jaxpr/ppermute | solution.py:14
  245.8 14.4 %collective-permute-start = (f32[8,64,128]{2,1,0:T(8,128)S(1)}, f32[8,64,128]{2,1,0:T(8,128)S(1)}, u32[]{:S(2)}, u32[]{:S(2)}) collective-permute-start(f32[8,64,128]{2,1,0:T(8,128)S(1)} %multiply_add_fusion.3), channel_id=1, source_target_pairs={{0,16},{16,32},{32,48},{48,64},{64,80},{80,96},{96,112},{112,128},... | collective-permute-start | bytes 786440 | tf_op jit(solution)/shard_map/while/body/eval_jaxpr/ppermute | solution.py:14
  272.2 0.7 copy-start.6
  272.2 200.5 %copy-start.1 = (bf16[32,4096]{1,0:T(8,128)(2,1)S(1)}, bf16[32,4096]{1,0:T(8,128)(2,1)}, u32[]{:S(2)}) copy-start(bf16[32,4096]{1,0:T(8,128)(2,1)} %param.27) | copy-start | bytes 786436
  272.2 201.8 %copy-start.4 = (f32[4096]{0:T(1024)S(1)}, f32[4096]{0:T(1024)}, u32[]{:S(2)}) copy-start(f32[4096]{0:T(1024)} %param.28) | copy-start | bytes 49156
  477.7 130.8 %all-to-all-start = ((bf16[16,32,4096]{2,1,0:T(8,128)(2,1)}), bf16[16,32,4096]{2,1,0:T(8,128)(2,1)}, u32[]{:S(2)}, u32[]{:S(2)}) async-start(bf16[16,32,4096]{2,1,0:T(8,128)(2,1)} %stack.2), calls=%async_computation.1 | async-start | bytes 8388608 | tf_op jit(solution)/shard_map/all_to_all | solution.py:120
  484.1 130.2 %all-gather.5.cloned.1.call-start = ((), (), s32[]{:S(2)}) async-start(), calls=%async_computation.5 | async-start | bytes 4456448 | tf_op jit(solution)/shard_map/all_gather | solution.py:79
  484.9 326.0 %reduce-scatter.5.cloned.1.call-start = ((), (), s32[]{:S(2)}) async-start(), calls=%async_computation.6 | async-start | bytes 8912896 | tf_op jit(solution)/shard_map/reduce_scatter | solution.py:125
  626.9 184.0 %copy-start = (f32[32,4096]{1,0:T(8,128)S(1)}, f32[32,4096]{1,0:T(8,128)}, u32[]{:S(2)}) copy-start(f32[32,4096]{1,0:T(8,128)} %reduce-scatter.3.cloned.1.call-done) | copy-start | bytes 1572868
Sparse Core Ops, SparseCore 0:
  9.9 89.6 all-gather.2
  272.4 200.3 reduce-scatter.2
  487.5 117.2 all-gather.4
  627.0 183.7 reduce-scatter.4
